TPU v7x, 32 devices: a whole 2x2x4 slice. The times are simulated.
32 devices in a mesh: heads: 4 (over y, core), seq: 8 (over z, x).
Axes of the slice: x: 2, y: 2, z: 4, core: 2. Of those that a mesh axis runs over, the one named last changes fastest.
Arguments:
- hidden: bfloat16 [8, 256, 2048], P('seq', 'heads'), may hold values from -6 to 6
- norm_gain: bfloat16 [2048], replicated, may hold values from 0.099609375 to 1.8984375
- router_weight: bfloat16 [2048, 4], replicated, may hold values from -0.125 to 0.125
- att_experts: int32 [8, 256, 2], P('seq'), may hold values from 0 to 3, all different within a row
- q_weight: bfloat16 [4, 2048, 1024], P(None, None, 'heads'), may hold values from -0.125 to 0.125
- kv_weight: bfloat16 [2, 2048, 1024], P(None, None, 'heads'), may hold values from -0.125 to 0.125
- o_weight: bfloat16 [4, 1024, 2048], P(None, 'heads'), may hold values from -1 to 1
- kv_cache: bfloat16 [2, 128, 128, 1024], P(None, 'seq', None, 'heads'), may hold values from -200 to 200
- cached_blocks: int32 [8], replicated, may hold values from 1 to 32, 128 in all
- tail_trim: int32 [8], replicated, may hold values from 0 to 127
- block_pool: int32 [128], replicated, may hold values from 0 to 127, each once
Outputs:
- attn_out: bfloat16 [8, 256, 2048], P('seq', 'heads')
Inputs may be any that keep to these rules, and one draw needn't show every extreme that they name: `block_pool`: the cached_blocks sum to 128, so every block belongs to one request.
All inputs are finite; a program needn't handle non-finite values.
Results may differ from a plain program's by a relative error of at most 0.019.
The roundings to bfloat16 on the way count: a program that leaves them out, or rounds other values in their place, can miss the bound.
Values may be sent and summed in bfloat16 or wider, within the bound.
No kernel may reach another device: no remote copies, remote signals or barrier semaphores. Data moves between devices by JAX's collectives and lax.ppermute only.
A program may use at most 128 MiB of HBM per device.

v0:
```python
import jax
import jax.numpy as jnp
from jax import lax
from jax.sharding import PartitionSpec as P

HD = 128
NEG_FILL = -1e30


def rotate(values, positions):
    half_dim = values.shape[-1] // 2
    inverse = 10000.0 ** (-2.0 * jnp.arange(half_dim, dtype=jnp.float32) / values.shape[-1])
    angles = positions.astype(jnp.float32)[:, None] * inverse[None, :]
    target = (values.shape[0],) + (1,) * (values.ndim - 2) + (half_dim,)
    cosine = jnp.cos(angles).reshape(target)
    sine_part = jnp.sin(angles).reshape(target)
    leading_part = values[..., :half_dim]
    trailing_part = values[..., half_dim:]
    return jnp.concatenate(
        [
            leading_part * cosine - trailing_part * sine_part,
            trailing_part * cosine + leading_part * sine_part,
        ],
        axis=-1,
    )


def normalize(rows, norm_gain):
    wide_rows = rows.astype(jnp.float32)
    scaled = wide_rows * lax.rsqrt(jnp.mean(wide_rows * wide_rows, axis=-1, keepdims=True) + 1e-05)
    return (scaled * norm_gain.astype(jnp.float32)).astype(jnp.bfloat16)


def route(normed, router_weight, chosen):
    logits = jnp.dot(normed, router_weight, preferred_element_type=jnp.float32)
    experts_all = router_weight.shape[1]
    onehot = (chosen[:, :, None] == jnp.arange(experts_all, dtype=jnp.int32)[None, None, :]).astype(
        jnp.float32
    )
    picked = jnp.sum(onehot * logits[:, None, :], axis=-1)
    return (onehot, jax.nn.softmax(picked, axis=-1))


def per_device(
    hidden,
    norm_gain,
    router_weight,
    att_experts,
    q_weight,
    kv_weight,
    o_weight,
    kv_cache,
    cached_blocks,
    tail_trim,
    block_pool,
):
    head_count = lax.axis_size("heads")
    seq_rank = lax.axis_index("seq")
    block_size = kv_cache.shape[2]
    local_blocks = kv_cache.shape[1]
    local_heads = q_weight.shape[2] // HD
    scale_q = HD ** (-0.5)
    normed = normalize(hidden[0], norm_gain)
    gathered = lax.all_gather(normed, "heads", axis=0, tiled=True)
    new_count = gathered.shape[0]
    chosen = att_experts[0]
    cached_len = cached_blocks * block_size - tail_trim
    positions = cached_len[seq_rank] + jnp.arange(new_count, dtype=jnp.int32)
    onehot, gates = route(gathered, router_weight, chosen)
    every_q = jnp.einsum("nd,edc->nec", gathered, q_weight, preferred_element_type=jnp.float32)
    chosen_q = jnp.sum(onehot[:, :, :, None] * every_q[:, None, :, :], axis=2).reshape(
        new_count, 2, local_heads, HD
    )
    queries = rotate(chosen_q, positions).astype(jnp.bfloat16)
    fresh = jnp.einsum("nd,sdc->snc", gathered, kv_weight, preferred_element_type=jnp.float32)
    new_keys = rotate(fresh[0].reshape(new_count, local_heads, HD), positions).astype(jnp.bfloat16)
    new_values = fresh[1].reshape(new_count, local_heads, HD).astype(jnp.bfloat16)
    all_queries = lax.all_gather(queries[None], "seq", axis=0, tiled=True)
    request_count = all_queries.shape[0]
    pool_size = block_pool.shape[0]
    global_ids = seq_rank * local_blocks + jnp.arange(local_blocks, dtype=jnp.int32)
    matches = block_pool[None, :] == global_ids[:, None]
    slot_of = jnp.sum(
        jnp.where(matches, jnp.arange(pool_size, dtype=jnp.int32)[None, :], 0), axis=1
    )
    starts = jnp.cumsum(cached_blocks) - cached_blocks
    owner = jnp.sum((starts[None, :] <= slot_of[:, None]).astype(jnp.int32), axis=1) - 1
    ordinal = slot_of - starts[owner]
    stat_shape = (request_count, new_count, 2, local_heads)
    initial = (
        jnp.full(stat_shape, NEG_FILL, jnp.float32),
        jnp.zeros(stat_shape, jnp.float32),
        jnp.zeros(stat_shape + (HD,), jnp.float32),
    )

    def visit(carry, block):
        best, totals, accum = carry
        request = owner[block]
        query_rows = lax.dynamic_index_in_dim(all_queries, request, 0, keepdims=False)
        pair_kv = lax.dynamic_index_in_dim(kv_cache, block, 1, keepdims=False)
        keys_here = pair_kv[0].reshape(block_size, local_heads, HD)
        values_here = pair_kv[1].reshape(block_size, local_heads, HD)
        scores = (
            jnp.einsum("nkhc,thc->nkht", query_rows, keys_here, preferred_element_type=jnp.float32)
            * scale_q
        )
        key_pos = ordinal[block] * block_size + jnp.arange(block_size, dtype=jnp.int32)
        scores = jnp.where((key_pos < cached_len[request])[None, None, None, :], scores, NEG_FILL)
        old_best = lax.dynamic_index_in_dim(best, request, 0, keepdims=False)
        new_best = jnp.maximum(old_best, jnp.max(scores, axis=-1))
        weights = jnp.exp(scores - new_best[..., None])
        rescale = jnp.exp(old_best - new_best)
        new_total = lax.dynamic_index_in_dim(
            totals, request, 0, keepdims=False
        ) * rescale + jnp.sum(weights, axis=-1)
        product = jnp.einsum(
            "nkht,thc->nkhc",
            weights.astype(jnp.bfloat16),
            values_here,
            preferred_element_type=jnp.float32,
        )
        new_accum = (
            lax.dynamic_index_in_dim(accum, request, 0, keepdims=False) * rescale[..., None]
            + product
        )
        best = lax.dynamic_update_index_in_dim(best, new_best, request, 0)
        totals = lax.dynamic_update_index_in_dim(totals, new_total, request, 0)
        accum = lax.dynamic_update_index_in_dim(accum, new_accum, request, 0)
        return ((best, totals, accum), None)

    scanned = lax.scan(visit, initial, jnp.arange(local_blocks, dtype=jnp.int32))
    best, totals, accum = scanned[0]
    self_scores = (
        jnp.einsum("nkhc,thc->nkht", queries, new_keys, preferred_element_type=jnp.float32)
        * scale_q
    )
    causal = (
        jnp.arange(new_count, dtype=jnp.int32)[None, :]
        <= jnp.arange(new_count, dtype=jnp.int32)[:, None]
    )
    self_scores = jnp.where(causal[:, None, None, :], self_scores, NEG_FILL)
    self_best = jnp.max(self_scores, axis=-1)
    self_weights = jnp.exp(self_scores - self_best[..., None])
    self_total = jnp.sum(self_weights, axis=-1)
    self_accum = jnp.einsum(
        "nkht,thc->nkhc",
        self_weights.astype(jnp.bfloat16),
        new_values,
        preferred_element_type=jnp.float32,
    )
    global_best = lax.pmax(best.astype(jnp.bfloat16), "seq").astype(best.dtype)
    factor = jnp.exp(best - global_best)
    cache_accum, cache_total = (
        lax.psum_scatter(
            (accum * factor[..., None]).astype(jnp.bfloat16), "seq", scatter_dimension=0, tiled=True
        ).astype(jnp.float32),
        lax.psum_scatter(
            (totals * factor).astype(jnp.bfloat16), "seq", scatter_dimension=0, tiled=True
        ).astype(jnp.float32),
    )
    cache_best = lax.dynamic_index_in_dim(global_best, seq_rank, 0, keepdims=True)
    peak = jnp.maximum(cache_best[0], self_best)
    cache_share = jnp.exp(cache_best[0] - peak)
    self_share = jnp.exp(self_best - peak)
    numerator = cache_accum[0] * cache_share[..., None] + self_accum * self_share[..., None]
    denominator = cache_total[0] * cache_share + self_total * self_share
    attended = (
        (numerator / denominator[..., None])
        .astype(jnp.bfloat16)
        .reshape(new_count, 2, local_heads * HD)
    )
    rows_each = new_count // head_count
    output = jnp.zeros((rows_each * lax.axis_size("heads"), o_weight.shape[2]), jnp.float32)
    for expert in range(o_weight.shape[0]):
        weight_expert = jnp.sum(onehot[:, :, expert] * gates, axis=1)
        picked = jnp.where(
            chosen[:, 0:1] == expert,
            attended[:, 0],
            jnp.where(chosen[:, 1:2] == expert, attended[:, 1], jnp.zeros_like(attended[:, 0])),
        )
        output = output + weight_expert[:, None] * jnp.dot(
            picked, o_weight[expert], preferred_element_type=jnp.float32
        )
    summed = lax.psum_scatter(
        output.astype(jnp.bfloat16), "heads", scatter_dimension=0, tiled=True
    ).astype(jnp.float32)
    return summed[None].astype(jnp.bfloat16)


def solution(mesh):
    return jax.shard_map(
        per_device,
        mesh=mesh,
        in_specs=(
            P("seq", "heads", None),
            P(),
            P(),
            P("seq", None, None),
            P(None, None, "heads"),
            P(None, None, "heads"),
            P(None, "heads", None),
            P(None, "seq", None, "heads"),
            P(),
            P(),
            P(),
        ),
        out_specs=P("seq", "heads", None),
        check_vma=False,
    )
```

profile of v0, /device:TPU:0, one launch (start us, length us, event | category | flops | bytes accessed | tf_op | source)
XLA Modules:
  0.0 434.2 jit_solution(16295591473125909563)
XLA Ops:
  7.4 1.1 fusion.35
  8.5 1.8 fusion.37
  14.0 1.2 multiply_cosine_fusion
  15.1 14.8 %all-gather.3.cloned.1.call-done = bf16[256,2048]{1,0:T(8,128)(2,1)} async-done(((bf16[64,2048]{1,0:T(8,128)(2,1)}), bf16[256,2048]{1,0:T(8,128)(2,1)}) %all-gather.3.cloned.1.call-update) | async-done | bytes 1048592 | tf_op jit(solution)/shard_map/all_gather | solution.py:64
  29.9 3.8 fusion.27
  38.4 48.4 %all-gather.5.cloned.1.call-done = bf16[8,256,2,2,128]{4,1,3,2,0:T(8,128)(2,1)} async-done(((bf16[1,256,2,2,128]{4,1,3,2,0:T(8,128)(2,1)}), bf16[8,256,2,2,128]{4,1,3,2,0:T(8,128)(2,1)}) %all-gather.5.cloned.1.call-update) | async-done | bytes 2097168 | tf_op jit(solution)/shard_map/all_gather | solution.py:78
  86.8 2.4 broadcast_in_dim.133
  89.2 202.3 %while.14 = (s32[]{:T(128)}, f32[8,256,2,2]{1,2,3,0:T(2,128)S(1)}, f32[8,256,2,2]{1,2,3,0:T(2,128)S(1)}, f32[8,256,2,2,128]{1,4,2,3,0:T(8,128)}, s32[16]{0:T(128...) while((s32[]{:T(128)}, f32[8,256,2,2]{1,2,3,0:T(2,128)S(1)}, ...), condition=%wide.region_12.13_spmd, body=%wide.region_9.12_spmd.sunk | while | flops 68292872 | bytes 4649549 | solution.py:131
  98.2 1.2 fusion.122
  99.7 1.1 constant_dynamic-slice_fusion.12
  110.9 1.2 fusion.122
  112.4 1.1 constant_dynamic-slice_fusion.12
  123.5 1.2 fusion.122
  125.0 1.1 constant_dynamic-slice_fusion.12
  136.1 1.2 fusion.122
  137.6 1.1 constant_dynamic-slice_fusion.12
  148.8 1.2 fusion.122
  150.3 1.1 constant_dynamic-slice_fusion.12
  161.4 1.2 fusion.122
  162.9 1.1 constant_dynamic-slice_fusion.12
  174.1 1.2 fusion.122
  175.6 1.1 constant_dynamic-slice_fusion.12
  186.7 1.2 fusion.122
  188.2 1.1 constant_dynamic-slice_fusion.12
  199.4 1.2 fusion.122
  200.9 1.1 constant_dynamic-slice_fusion.12
  212.0 1.2 fusion.122
  213.5 1.1 constant_dynamic-slice_fusion.12
  224.6 1.2 fusion.122
  237.3 1.2 fusion.122
  249.9 1.2 fusion.122
  262.6 1.2 fusion.122
  264.1 1.1 constant_dynamic-slice_fusion.12
  275.2 1.2 fusion.122
  287.8 1.2 fusion.122
  289.4 1.1 constant_dynamic-slice_fusion.12
  291.5 34.7 %pmax.7 = bf16[8,256,2,2]{1,2,3,0:T(2,128)(2,1)S(1)} all-reduce(bf16[8,256,2,2]{1,2,3,0:T(2,128)(2,1)S(1)} %convert_element_type.81), channel_id=1, replica_groups=mesh['heads'=4,'seq'=8] {'seq'}, use_global_device_ids=true, to_apply=%region_13.14 | all-reduce | flops 8192 | bytes 32768 | tf_op jit(solution)/shard_map/pmax | solution.py:151
  326.8 4.0 multiply_convert_fusion
  330.9 1.3 dynamic-slice
  332.3 1.4 compare_reduce_fusion.1
  336.3 1.6 fusion.103
  338.7 1.4 fusion.102
  340.3 33.7 %all-reduce = bf16[8,256,2,2]{1,2,3,0:T(2,128)(2,1)S(1)} all-reduce(bf16[8,256,2,2]{1,2,3,0:T(2,128)(2,1)} %get-tuple-element.139), channel_id=3, replica_groups=mesh['heads'=4,'seq'=8] {'seq'}, use_global_device_ids=true, to_apply=%region_16.17.clone | all-reduce | flops 8192 | bytes 32768
  374.5 22.9 %reduce-scatter.3.cloned.1.call-done = bf16[1,256,2,2,128]{1,4,2,3,0:T(8,128)(2,1)} async-done(((bf16[8,256,2,2,128]{1,4,2,3,0:T(8,128)(2,1)}), bf16[1,256,2,2,128]{1,4,2,3,0:T(8,128)(2,1)}) %reduce-scatter.3.cloned.1.call-update) | async-done | bytes 262160 | tf_op jit(solution)/shard_map/reduce_scatter | solution.py:154
  397.5 1.5 fusion.21
  399.0 1.7 convolution_multiply_fusion.4
  402.1 1.5 fusion.15
  403.6 24.0 %reduce-scatter.5.cloned.1.call-done = bf16[64,2048]{1,0:T(8,128)(2,1)} async-done(((bf16[256,2048]{1,0:T(8,128)(2,1)}), bf16[64,2048]{1,0:T(8,128)(2,1)}) %reduce-scatter.5.cloned.1.call-update) | async-done | bytes 262160 | tf_op jit(solution)/shard_map/reduce_scatter | solution.py:184
  (296 shorter events, 108.7 us)
Async XLA Ops:
  6.5 327.8 %copy-start = (bf16[2,2048,256]{2,1,0:T(8,128)(2,1)S(1)}, bf16[2,2048,256]{2,1,0:T(8,128)(2,1)}, u32[]{:S(2)}) copy-start(bf16[2,2048,256]{2,1,0:T(8,128)(2,1)} %param.18) | copy-start | bytes 6291460
  6.5 23.4 %all-gather.3.cloned.1.call-start = ((), (), s32[]{:S(2)}) async-start(), calls=%async_computation.2 | async-start | bytes 1310720 | tf_op jit(solution)/shard_map/all_gather | solution.py:64
  10.3 76.5 %all-gather.5.cloned.1.call-start = ((), (), s32[]{:S(2)}) async-start(), calls=%async_computation.3 | async-start | bytes 2359296 | tf_op jit(solution)/shard_map/all_gather | solution.py:78
  11.1 2.2 copy-start.5
  34.4 2.9 copy-start.21
  35.7 0.7 copy-start.2
  37.3 360.1 %reduce-scatter.3.cloned.1.call-start = ((), (), s32[]{:S(2)}) async-start(), calls=%async_computation.4 | async-start | bytes 2359296 | tf_op jit(solution)/shard_map/reduce_scatter | solution.py:154
  330.9 3.4 copy-start.4
  330.9 96.7 %reduce-scatter.5.cloned.1.call-start = ((), (), s32[]{:S(2)}) async-start(), calls=%async_computation.5 | async-start | bytes 1310720 | tf_op jit(solution)/shard_map/reduce_scatter | solution.py:184
  335.2 1.0 copy-start.8
  335.2 2.6 copy-start.7
  335.3 2.7 copy-start.6
  335.3 3.3 copy-start.3
  340.2 58.8 %copy-start.11 = (f32[256]{0:T(256)S(1)}, f32[256]{0:T(256)}, u32[]{:S(2)}) copy-start(f32[256]{0:T(256)} %get-tuple-element.105) | copy-start | bytes 3076
  340.2 58.8 %copy-start.17 = (pred[256]{0:T(512)(128)(4,1)S(1)}, pred[256]{0:T(512)(128)(4,1)}, u32[]{:S(2)}) copy-start(pred[256]{0:T(512)(128)(4,1)} %get-tuple-element.112) | copy-start | bytes 772
  340.2 58.8 %copy-start.18 = (pred[256]{0:T(512)(128)(4,1)S(1)}, pred[256]{0:T(512)(128)(4,1)}, u32[]{:S(2)}) copy-start(pred[256]{0:T(512)(128)(4,1)} %get-tuple-element.113) | copy-start | bytes 772
  397.5 3.3 copy-start.1
  398.9 1.8 copy-start.10
  399.0 1.8 copy-start.15
  399.0 1.8 copy-start.16
  400.8 0.7 copy-start.9
  400.8 0.7 copy-start.13
  400.8 0.6 copy-start.14
  401.4 0.6 copy-start.12
  401.4 0.7 copy-start.19
  401.4 0.7 copy-start.20
Sparse Core Ops, SparseCore 0:
  10.4 19.4 all-gather.2
  37.4 49.2 all-gather.4
  331.0 66.3 reduce-scatter.2
  403.7 23.8 reduce-scatter.4
where the time goes:
time: 438 us; the launch traced here: 434 us
  waiting for transfers between devices  110 us (25%)
  local copies, waits for them, and re-layouts  84.8 us (19%)
  loops' own time  76 us (17%)
  blocking collectives  68.3 us (16%)
  matrix products  49.9 us (11%)
  other arithmetic  31.2 us (7%)
  between operations  13.6 us (3%)
    another operation x1, loops' own time, per_device(): lax.scan(visit, initial, jnp.arange(local_blocks, dtype=jnp.int32))  76 us
    all_gather x1, waiting for transfers between devices, per_device(): all_queries = lax.all_gather(queries[None], 'seq', axis=0, tiled=True)  48.4 us
    pmax x1, blocking collectives, per_device(): global_best = lax.pmax(best.astype(jnp.bfloat16), 'seq').astype(best.dtype)  34.7 us
    unnamed x1, blocking collectives  33.7 us
    reduce_scatter x1, waiting for transfers between devices, per_device(): lax.psum_scatter(output.astype(jnp.bfloat16), 'heads', scatter_dimension=...  24 us
    reduce_scatter x1, waiting for transfers between devices, per_device(): lax.psum_scatter((accum * factor[..., None]).astype(jnp.bfloat16), 'seq',...  22.9 us
    dot_general x16, matrix products, visit(): jnp.einsum('nkhc,thc->nkht', query_rows, keys_here, preferred_element_typ...  19.8 us
    dynamic_slice x16, local copies, waits for them, and re-layouts, visit(): lax.dynamic_index_in_dim(accum, request, 0, keepdims=False)  17.3 us
  transfers between devices with their start and end apart: 4, of which 4 were waited for; matrix products, arithmetic and copies ran while one was open for 4% of the time, Pallas kernels for 0%

commit v1 on v0

--- a/solution.py
+++ b/solution.py
@@ -75,7 +75,17 @@
     fresh = jnp.einsum("nd,sdc->snc", gathered, kv_weight, preferred_element_type=jnp.float32)
     new_keys = rotate(fresh[0].reshape(new_count, local_heads, HD), positions).astype(jnp.bfloat16)
     new_values = fresh[1].reshape(new_count, local_heads, HD).astype(jnp.bfloat16)
-    all_queries = lax.all_gather(queries[None], "seq", axis=0, tiled=True)
+    view = queries[None]
+    count_all = jax.lax.axis_size("seq")
+    current_arr = sorted(((dev, (dev + 1) % count_all) for dev in range(count_all)))
+    low = view
+    block_list = [low]
+    for b in tuple(range(1, count_all)):
+        low = jax.lax.ppermute(low, "seq", current_arr)
+        block_list.insert(0, low)
+    all_queries = jnp.roll(
+        jnp.concatenate(block_list, axis=0), (jax.lax.axis_index("seq") + 1) * view.shape[0], axis=0
+    )
     request_count = all_queries.shape[0]
     pool_size = block_pool.shape[0]
     global_ids = seq_rank * local_blocks + jnp.arange(local_blocks, dtype=jnp.int32)

time: 438 us -> 457 us (1.043)
  waiting for transfers between devices: 110 us -> 124 us
  local copies, waits for them, and re-layouts: 84.8 us -> 91.7 us
    ppermute x0 -> x7, waiting for transfers between devices: none -> 65.9 us  [per_device(): low = jax.lax.ppermute(low, 'seq', current_arr)]
    all_gather x1 -> x0, waiting for transfers between devices: 48.4 us -> none  [per_device(): all_queries = lax.all_gather(queries[None], 'seq', axis=0, tiled=True)]
    unnamed x49 -> x59, local copies, waits for them, and re-layouts: 3.06 us -> 12.8 us
  transfers between devices with their start and end apart: 4 -> 10, of which waited for: 4 -> 10; matrix products, arithmetic and copies ran while one was open for 4% -> 3% of each run, Pallas kernels for 0% -> 0%
where the time goes in v1:
time: 457 us; the launch traced here: 453 us
  waiting for transfers between devices  124 us (27%)
  local copies, waits for them, and re-layouts  91.7 us (20%)
  loops' own time  73.3 us (16%)
  blocking collectives  66.6 us (15%)
  matrix products  51.5 us (11%)
  other arithmetic  30.5 us (7%)
  between operations  13.7 us (3%)
    another operation x1, loops' own time, per_device(): lax.scan(visit, initial, jnp.arange(local_blocks, dtype=jnp.int32))  73.3 us
    ppermute x7, waiting for transfers between devices, per_device(): low = jax.lax.ppermute(low, 'seq', current_arr)  65.9 us
    unnamed x1, blocking collectives  33.6 us
    pmax x1, blocking collectives, per_device(): global_best = lax.pmax(best.astype(jnp.bfloat16), 'seq').astype(best.dtype)  33 us
    reduce_scatter x1, waiting for transfers between devices, per_device(): lax.psum_scatter(output.astype(jnp.bfloat16), 'heads', scatter_dimension=...  24 us
    dot_general x16, matrix products, visit(): jnp.einsum('nkhc,thc->nkht', query_rows, keys_here, preferred_element_typ...  19.8 us
    reduce_scatter x1, waiting for transfers between devices, per_device(): lax.psum_scatter((accum * factor[..., None]).astype(jnp.bfloat16), 'seq',...  19 us
    dynamic_slice x16, local copies, waits for them, and re-layouts, visit(): lax.dynamic_index_in_dim(accum, request, 0, keepdims=False)  17.3 us
  transfers between devices with their start and end apart: 10, of which 10 were waited for; matrix products, arithmetic and copies ran while one was open for 3% of the time, Pallas kernels for 0%

profile of v1, /device:TPU:0, one launch (start us, length us, event | category | flops | bytes accessed | tf_op | source)
XLA Modules:
  0.0 453.4 jit_solution(16411925639068010212)
XLA Ops:
  6.5 1.2 fusion.38
  8.5 1.8 fusion.40
  14.5 15.4 %all-gather.2.cloned.1.call-done = bf16[256,2048]{1,0:T(8,128)(2,1)} async-done(((bf16[64,2048]{1,0:T(8,128)(2,1)}), bf16[256,2048]{1,0:T(8,128)(2,1)}) %all-gather.2.cloned.1.call-update) | async-done | bytes 1048592 | tf_op jit(solution)/shard_map/all_gather | solution.py:64
  29.9 3.8 fusion.30
  35.5 1.2 subtract_convert_fusion
  36.9 1.5 collective-permute-start
  38.4 9.7 %collective-permute-done = bf16[1,256,2,2,128]{4,1,2,3,0:T(8,128)(2,1)S(1)} collective-permute-done((bf16[1,256,2,2,128]{4,1,2,3,0:T(8,128)(2,1)S(1)}, bf16[1,256,2,2,128]{4,1,2,3,0:T(8,128)(2,1)S(1)}, u32[]{:S(2)}, u32[]{:S(2)}) %collective-permute-start) | collective-permute-done | bytes 262176 | tf_op jit(solution)/shard_map/ppermute | solution.py:84
  48.0 10.3 %collective-permute-done.1 = bf16[1,256,2,2,128]{4,1,2,3,0:T(8,128)(2,1)S(1)} collective-permute-done((bf16[1,256,2,2,128]{4,1,2,3,0:T(8,128)(2,1)S(1)}, bf16[1,256,2,2,128]{4,1,2,3,0:T(8,128)(2,1)S(1)}, u32[]{:S(2)}, u32[]{:S(2)}) %collective-permute-start.1) | collective-permute-done | bytes 262176 | tf_op jit(solution)/shard_map/ppermute | solution.py:84
  58.4 9.4 %collective-permute-done.2 = bf16[1,256,2,2,128]{4,1,2,3,0:T(8,128)(2,1)S(1)} collective-permute-done((bf16[1,256,2,2,128]{4,1,2,3,0:T(8,128)(2,1)S(1)}, bf16[1,256,2,2,128]{4,1,2,3,0:T(8,128)(2,1)S(1)}, u32[]{:S(2)}, u32[]{:S(2)}) %collective-permute-start.2) | collective-permute-done | bytes 262176 | tf_op jit(solution)/shard_map/ppermute | solution.py:84
  68.5 9.2 %collective-permute-done.3 = bf16[1,256,2,2,128]{4,1,2,3,0:T(8,128)(2,1)} collective-permute-done((bf16[1,256,2,2,128]{4,1,2,3,0:T(8,128)(2,1)S(1)}, bf16[1,256,2,2,128]{4,1,2,3,0:T(8,128)(2,1)}, u32[]{:S(2)}, u32[]{:S(2)}) %collective-permute-start.3) | collective-permute-done | bytes 262176 | tf_op jit(solution)/shard_map/ppermute | solution.py:84
  77.8 9.2 %collective-permute-done.4 = bf16[1,256,2,2,128]{4,1,2,3,0:T(8,128)(2,1)} collective-permute-done((bf16[1,256,2,2,128]{4,1,2,3,0:T(8,128)(2,1)}, bf16[1,256,2,2,128]{4,1,2,3,0:T(8,128)(2,1)}, u32[]{:S(2)}, u32[]{:S(2)}) %collective-permute-start.4) | collective-permute-done | bytes 262176 | tf_op jit(solution)/shard_map/ppermute | solution.py:84
  87.1 9.5 %collective-permute-done.5 = bf16[1,256,2,2,128]{4,1,2,3,0:T(8,128)(2,1)} collective-permute-done((bf16[1,256,2,2,128]{4,1,2,3,0:T(8,128)(2,1)}, bf16[1,256,2,2,128]{4,1,2,3,0:T(8,128)(2,1)}, u32[]{:S(2)}, u32[]{:S(2)}) %collective-permute-start.5) | collective-permute-done | bytes 262176 | tf_op jit(solution)/shard_map/ppermute | solution.py:84
  97.3 8.7 %collective-permute-done.6 = bf16[1,256,2,2,128]{4,1,2,3,0:T(8,128)(2,1)} collective-permute-done((bf16[1,256,2,2,128]{4,1,2,3,0:T(8,128)(2,1)}, bf16[1,256,2,2,128]{4,1,2,3,0:T(8,128)(2,1)}, u32[]{:S(2)}, u32[]{:S(2)}) %collective-permute-start.6) | collective-permute-done | bytes 262176 | tf_op jit(solution)/shard_map/ppermute | solution.py:84
  115.5 1.5 constant_dynamic-slice_fusion.4
  117.0 2.4 broadcast_in_dim.133
  119.4 195.5 %while.14 = (s32[]{:T(128)}, f32[8,256,2,2]{1,2,3,0:T(2,128)S(1)}, f32[8,256,2,2]{1,2,3,0:T(2,128)S(1)}, f32[8,256,2,2,128]{1,4,2,3,0:T(8,128)}, s32[16]{0:T(128...) while((s32[]{:T(128)}, f32[8,256,2,2]{1,2,3,0:T(2,128)S(1)}, ...), condition=%wide.region_12.13_spmd, body=%wide.region_9.12_spmd.sunk | while | flops 68292872 | bytes 4649549 | solution.py:141
  128.1 1.2 fusion.125
  129.5 1.1 constant_dynamic-slice_fusion.8
  140.3 1.2 fusion.125
  152.6 1.2 fusion.125
  164.8 1.2 fusion.125
  166.2 1.1 constant_dynamic-slice_fusion.8
  177.0 1.2 fusion.125
  178.4 1.1 constant_dynamic-slice_fusion.8
  189.2 1.2 fusion.125
  190.6 1.1 constant_dynamic-slice_fusion.8
  201.4 1.2 fusion.125
  202.8 1.1 constant_dynamic-slice_fusion.8
  213.7 1.2 fusion.125
  225.9 1.2 fusion.125
  238.1 1.2 fusion.125
  250.3 1.2 fusion.125
  262.6 1.2 fusion.125
  274.8 1.2 fusion.125
  287.0 1.2 fusion.125
  299.2 1.2 fusion.125
  311.4 1.2 fusion.125
  315.0 33.0 %pmax.7 = bf16[8,256,2,2]{1,2,3,0:T(2,128)(2,1)S(1)} all-reduce(bf16[8,256,2,2]{1,2,3,0:T(2,128)(2,1)S(1)} %convert_element_type.81), channel_id=1, replica_groups=mesh['heads'=4,'seq'=8] {'seq'}, use_global_device_ids=true, to_apply=%region_13.14 | all-reduce | flops 8192 | bytes 32768 | tf_op jit(solution)/shard_map/pmax | solution.py:161
  348.6 4.0 multiply_convert_fusion
  354.7 2.2 convolution_bitcast_fusion.2
  357.8 1.6 fusion.106
  360.2 1.3 fusion.105
  363.4 33.6 %all-reduce = bf16[8,256,2,2]{1,2,3,0:T(2,128)(2,1)S(1)} all-reduce(bf16[8,256,2,2]{1,2,3,0:T(2,128)(2,1)} %get-tuple-element.139), channel_id=3, replica_groups=mesh['heads'=4,'seq'=8] {'seq'}, use_global_device_ids=true, to_apply=%region_16.17.clone | all-reduce | flops 8192 | bytes 32768
  397.7 19.0 %reduce-scatter.3.cloned.1.call-done = bf16[1,256,2,2,128]{1,4,2,3,0:T(8,128)(2,1)} async-done(((bf16[8,256,2,2,128]{1,4,2,3,0:T(8,128)(2,1)}), bf16[1,256,2,2,128]{1,4,2,3,0:T(8,128)(2,1)}) %reduce-scatter.3.cloned.1.call-update) | async-done | bytes 262160 | tf_op jit(solution)/shard_map/reduce_scatter | solution.py:164
  416.7 1.7 fusion.24
  418.5 1.7 convolution_multiply_fusion.4
  421.3 1.5 fusion.18
  422.8 24.0 %reduce-scatter.5.cloned.1.call-done = bf16[64,2048]{1,0:T(8,128)(2,1)} async-done(((bf16[256,2048]{1,0:T(8,128)(2,1)}), bf16[64,2048]{1,0:T(8,128)(2,1)}) %reduce-scatter.5.cloned.1.call-update) | async-done | bytes 262160 | tf_op jit(solution)/shard_map/reduce_scatter | solution.py:194
  (319 shorter events, 122.7 us)
Async XLA Ops:
  6.5 348.1 %copy-start = (bf16[2,2048,256]{2,1,0:T(8,128)(2,1)S(1)}, bf16[2,2048,256]{2,1,0:T(8,128)(2,1)}, u32[]{:S(2)}) copy-start(bf16[2,2048,256]{2,1,0:T(8,128)(2,1)} %param.18) | copy-start | bytes 6291460
  6.5 23.4 %all-gather.2.cloned.1.call-start = ((), (), s32[]{:S(2)}) async-start(), calls=%async_computation.2 | async-start | bytes 1310720 | tf_op jit(solution)/shard_map/all_gather | solution.py:64
  10.3 406.4 %reduce-scatter.3.cloned.1.call-start = ((), (), s32[]{:S(2)}) async-start(), calls=%async_computation.3 | async-start | bytes 2359296 | tf_op jit(solution)/shard_map/reduce_scatter | solution.py:164
  33.7 44.0 %copy-start.18 = (s32[128]{0:T(128)S(1)}, s32[128]{0:T(128)}, u32[]{:S(2)}) copy-start(s32[128]{0:T(128)} %param.23) | copy-start | bytes 1540
  36.9 11.2 %collective-permute-start = (bf16[1,256,2,2,128]{4,1,2,3,0:T(8,128)(2,1)S(1)}, bf16[1,256,2,2,128]{4,1,2,3,0:T(8,128)(2,1)S(1)}, u32[]{:S(2)}, u32[]{:S(2)}) collective-permute-start(bf16[1,256,2,2,128]{4,1,2,3,0:T(8,128)(2,1)S(1)} %pad_maximum_fusion), channel_id=1, source_target_pairs={{0,1},{1,2},{2,3},{3,4},{4,5},{5,6},{6,7},{7,0},{8,9},{9,10},{10,1... | collective-permute-start | bytes 786440 | tf_op jit(solution)/shard_map/ppermute | solution.py:84
  48.0 10.3 %collective-permute-start.1 = (bf16[1,256,2,2,128]{4,1,2,3,0:T(8,128)(2,1)S(1)}, bf16[1,256,2,2,128]{4,1,2,3,0:T(8,128)(2,1)S(1)}, u32[]{:S(2)}, u32[]{:S(2)}) collective-permute-start(bf16[1,256,2,2,128]{4,1,2,3,0:T(8,128)(2,1)S(1)} %collective-permute-done), channel_id=1, source_target_pairs={{0,1},{1,2},{2,3},{3,4},{4,5},{5,6},{6,7},{7,0},{8,9},{9,10},{10,1... | collective-permute-start | bytes 786440 | tf_op jit(solution)/shard_map/ppermute | solution.py:84
  58.4 9.4 %collective-permute-start.2 = (bf16[1,256,2,2,128]{4,1,2,3,0:T(8,128)(2,1)S(1)}, bf16[1,256,2,2,128]{4,1,2,3,0:T(8,128)(2,1)S(1)}, u32[]{:S(2)}, u32[]{:S(2)}) collective-permute-start(bf16[1,256,2,2,128]{4,1,2,3,0:T(8,128)(2,1)S(1)} %collective-permute-done.1), channel_id=1, source_target_pairs={{0,1},{1,2},{2,3},{3,4},{4,5},{5,6},{6,7},{7,0},{8,9},{9,10},{10,1... | collective-permute-start | bytes 786440 | tf_op jit(solution)/shard_map/ppermute | solution.py:84
  67.8 0.7 copy-start.3
  68.5 9.2 %collective-permute-start.3 = (bf16[1,256,2,2,128]{4,1,2,3,0:T(8,128)(2,1)S(1)}, bf16[1,256,2,2,128]{4,1,2,3,0:T(8,128)(2,1)}, u32[]{:S(2)}, u32[]{:S(2)}) collective-permute-start(bf16[1,256,2,2,128]{4,1,2,3,0:T(8,128)(2,1)S(1)} %collective-permute-done.2), channel_id=1, source_target_pairs={{0,1},{1,2},{2,3},{3,4},{4,5},{5,6},{6,7},{7,0},{8,9},{9,10},{10,1... | collective-permute-start | bytes 786440 | tf_op jit(solution)/shard_map/ppermute | solution.py:84
  77.6 9.4 %collective-permute-start.4 = (bf16[1,256,2,2,128]{4,1,2,3,0:T(8,128)(2,1)}, bf16[1,256,2,2,128]{4,1,2,3,0:T(8,128)(2,1)}, u32[]{:S(2)}, u32[]{:S(2)}) collective-permute-start(bf16[1,256,2,2,128]{4,1,2,3,0:T(8,128)(2,1)} %collective-permute-done.3), channel_id=1, source_target_pairs={{0,1},{1,2},{2,3},{3,4},{4,5},{5,6},{6,7},{7,0},{8,9},{9,10},{10,1... | collective-permute-start | bytes 786440 | tf_op jit(solution)/shard_map/ppermute | solution.py:84
  87.0 9.6 %collective-permute-start.5 = (bf16[1,256,2,2,128]{4,1,2,3,0:T(8,128)(2,1)}, bf16[1,256,2,2,128]{4,1,2,3,0:T(8,128)(2,1)}, u32[]{:S(2)}, u32[]{:S(2)}) collective-permute-start(bf16[1,256,2,2,128]{4,1,2,3,0:T(8,128)(2,1)} %collective-permute-done.4), channel_id=1, source_target_pairs={{0,1},{1,2},{2,3},{3,4},{4,5},{5,6},{6,7},{7,0},{8,9},{9,10},{10,1... | collective-permute-start | bytes 786440 | tf_op jit(solution)/shard_map/ppermute | solution.py:84
  96.6 9.4 %collective-permute-start.6 = (bf16[1,256,2,2,128]{4,1,2,3,0:T(8,128)(2,1)}, bf16[1,256,2,2,128]{4,1,2,3,0:T(8,128)(2,1)}, u32[]{:S(2)}, u32[]{:S(2)}) collective-permute-start(bf16[1,256,2,2,128]{4,1,2,3,0:T(8,128)(2,1)} %collective-permute-done.5), channel_id=1, source_target_pairs={{0,1},{1,2},{2,3},{3,4},{4,5},{5,6},{6,7},{7,0},{8,9},{9,10},{10,1... | collective-permute-start | bytes 786440 | tf_op jit(solution)/shard_map/ppermute | solution.py:84
  97.3 17.9 %copy-start.4 = (bf16[1,256,2,2,128]{4,1,2,3,0:T(8,128)(2,1)S(1)}, bf16[1,256,2,2,128]{4,1,2,3,0:T(8,128)(2,1)}, u32[]{:S(2)}) copy-start(bf16[1,256,2,2,128]{4,1,2,3,0:T(8,128)(2,1)} %copy-done.3) | copy-start | bytes 786436
  348.0 4.7 %copy-start.5 = (bf16[8,256,2,2]{1,2,3,0:T(2,128)(2,1)}, bf16[8,256,2,2]{1,2,3,0:T(2,128)(2,1)S(1)}, u32[]{:S(2)}) copy-start(bf16[8,256,2,2]{1,2,3,0:T(2,128)(2,1)S(1)} %pmax.7) | copy-start | bytes 49156
  348.6 4.1 copy-start.19
  348.6 4.8 %copy-start.7 = (s32[1,256,2]{1,2,0:T(2,128)S(1)}, s32[1,256,2]{1,2,0:T(2,128)}, u32[]{:S(2)}) copy-start(s32[1,256,2]{1,2,0:T(2,128)} %param.16) | copy-start | bytes 6148
  352.7 94.1 %reduce-scatter.5.cloned.1.call-start = ((), (), s32[]{:S(2)}) async-start(), calls=%async_computation.4 | async-start | bytes 1310720 | tf_op jit(solution)/shard_map/reduce_scatter | solution.py:194
  357.8 58.9 %copy-start.6 = (bf16[1,256,256]{1,2,0:T(8,128)(2,1)S(1)}, bf16[1,256,256]{1,2,0:T(8,128)(2,1)}, u32[]{:S(2)}) copy-start(bf16[1,256,256]{1,2,0:T(8,128)(2,1)} %slice.186) | copy-start | bytes 393220
  360.2 58.3 %copy-start.10 = (f32[256]{0:T(256)S(1)}, f32[256]{0:T(256)}, u32[]{:S(2)}) copy-start(f32[256]{0:T(256)} %get-tuple-element.105) | copy-start | bytes 3076
  361.5 1.0 copy-start.2
  361.5 58.7 %copy-start.9 = (f32[256]{0:T(256)S(1)}, f32[256]{0:T(256)}, u32[]{:S(2)}) copy-start(f32[256]{0:T(256)} %get-tuple-element.104) | copy-start | bytes 3076
  361.5 58.7 %copy-start.14 = (pred[256]{0:T(512)(128)(4,1)S(1)}, pred[256]{0:T(512)(128)(4,1)}, u32[]{:S(2)}) copy-start(pred[256]{0:T(512)(128)(4,1)} %get-tuple-element.107) | copy-start | bytes 772
  361.5 58.7 %copy-start.15 = (pred[256]{0:T(512)(128)(4,1)S(1)}, pred[256]{0:T(512)(128)(4,1)}, u32[]{:S(2)}) copy-start(pred[256]{0:T(512)(128)(4,1)} %get-tuple-element.109) | copy-start | bytes 772
  416.7 3.6 copy-start.1
  418.5 2.3 copy-start.8
  418.5 2.3 copy-start.12
  418.5 2.3 copy-start.13
  420.3 1.0 copy-start.11
  420.3 1.0 copy-start.16
  420.3 1.0 copy-start.17
Sparse Core Ops, SparseCore 0:
  10.4 19.4 all-gather.1
  352.8 63.8 reduce-scatter.2
  422.9 23.8 reduce-scatter.4
